TPU v7x, 32 devices: a whole 2x2x4 slice. The times are simulated.
32 devices in a mesh: groups: 2 (over x), seq: 4 (over y, core), pair: 4 (over z).
Axes of the slice: x: 2, y: 2, z: 4, core: 2. Of those that a mesh axis runs over, the one named last changes fastest.
Arguments:
- sequence: bfloat16 [4096, 1536], P(('groups', 'seq', 'pair')), parts along dimension 0, may hold values from -12 to 12
- gain_conv: float32 [1536], replicated, may hold values from 0.25 to 1.75
- conv_weight: bfloat16 [5, 1536, 1536], P(None, 'pair'), may hold values from -0.0625 to 0.0625
- gain_attn: float32 [1536], replicated, may hold values from 0.25 to 1.75
- w_qkv: bfloat16 [1536, 3072], P(None, 'pair'), may hold values from -1 to 1
- w_out: bfloat16 [1024, 1536], P('pair'), may hold values from -0.75 to 0.75
- gain_pool: float32 [1536], replicated, may hold values from 0.25 to 1.75
- w_pair: bfloat16 [1536, 256], replicated, may hold values from -0.15625 to 0.15625
- w_up: bfloat16 [128, 256], replicated, may hold values from -0.5 to 0.5
- w_down: bfloat16 [256, 128], replicated, may hold values from -0.375 to 0.375
Outputs:
- seq_out: bfloat16 [4096, 1536], P(('groups', 'seq', 'pair')), parts along dimension 0
- pair_map: bfloat16 [256, 128, 128], P(('groups', 'seq'), 'pair'), parts along dimension 0
There are 2 independent parts, one for each index of `groups`. A program takes and returns all parts, laid end to end along the dimension named above; an argument that names none is the same for every part. Nothing has to cross between parts.
All inputs are finite; a program needn't handle non-finite values.
Results may differ from a plain program's by a relative error of at most 0.024.
Values may be sent and summed in bfloat16 or wider, within the bound.
No kernel may reach another device: no remote copies, remote signals or barrier semaphores. Data moves between devices by JAX's collectives and lax.ppermute only.
A program may use at most 64 MiB of HBM per device.

v0:
```python
import math
import jax
import jax.numpy as jnp
from jax import lax
from jax.sharding import PartitionSpec as P

KEY_SIZE = 128
VALUE_SIZE = 128
DILATION = 4
POOL = 16
PAIR_CH = 128
EPS = 1e-06


def padded_2(value, sides, width):
    for axis, dim in sides:
        peers, length = (lax.axis_size(axis), value.shape[dim])
        up = [(i, (i + 1) % peers) for i in range(peers - 1)]
        down = [(j, i) for i, j in up]
        last = lax.slice_in_dim(value, length - width, length, axis=dim)
        first = lax.slice_in_dim(value, 0, width, axis=dim)
        before = lax.ppermute(last, axis, up)
        after = lax.ppermute(first, axis, down)
        value = jnp.concatenate([before, value, after], axis=dim)
    return value


def norm_rows(values, gain):
    return values * lax.rsqrt(jnp.mean(values * values, axis=-1, keepdims=True) + EPS) * gain


def conv_rows(padded, conv_weight, row_total):
    summed = jnp.zeros((row_total, conv_weight.shape[2]), jnp.float32)
    for offset in range(conv_weight.shape[0]):
        shifted = lax.dynamic_slice_in_dim(padded, offset * DILATION, row_total, 0)
        summed = summed + jnp.dot(shifted, conv_weight[offset], preferred_element_type=jnp.float32)
    return summed


def shards(
    sequence, gain_conv, conv_weight, gain_attn, w_qkv, w_out, gain_pool, w_pair, w_up, w_down
):
    pair_count = lax.axis_size("pair")
    seq_count = lax.axis_size("seq")
    row_count = sequence.shape[0]
    channels = sequence.shape[1]
    local_rows = row_count * pair_count
    inputs = sequence.astype(jnp.float32)
    normed = norm_rows(inputs, gain_conv).astype(jnp.bfloat16)
    swapped = lax.all_to_all(normed, "pair", split_axis=1, concat_axis=0, tiled=True)
    padded = padded_2(swapped, (("seq", 0),), DILATION * (conv_weight.shape[0] - 1) // 2)
    summed = lax.psum_scatter(
        conv_rows(padded, conv_weight, row_count * lax.axis_size("pair")),
        "pair",
        scatter_dimension=0,
        tiled=True,
    )
    first_out = (inputs + summed).astype(jnp.bfloat16)
    attn_in = norm_rows(first_out.astype(jnp.float32), gain_attn).astype(jnp.bfloat16)
    projected = jnp.dot(
        lax.all_gather(attn_in, "pair", axis=0, tiled=True),
        w_qkv,
        preferred_element_type=jnp.float32,
    ).astype(jnp.bfloat16)
    head_count = projected.shape[1] // (2 * KEY_SIZE + VALUE_SIZE)
    grouped = projected.reshape(local_rows, head_count, 2 * KEY_SIZE + VALUE_SIZE)
    queries = grouped[:, :, :KEY_SIZE]
    key_rows = grouped[:, :, KEY_SIZE : 2 * KEY_SIZE].reshape(local_rows, head_count * KEY_SIZE)
    value_rows = grouped[:, :, 2 * KEY_SIZE :].reshape(local_rows, head_count * VALUE_SIZE)
    scale = 1.0 / math.sqrt(KEY_SIZE)
    start_state = (
        jnp.full((head_count, local_rows), -1e30, jnp.float32),
        jnp.zeros((head_count, local_rows), jnp.float32),
        jnp.zeros((head_count, local_rows, VALUE_SIZE), jnp.float32),
    )
    carried = start_state
    key_piece = lax.all_gather(key_rows, "seq", axis=0, tiled=True)
    value_piece = lax.all_gather(value_rows, "seq", axis=0, tiled=True)
    piece_rows = key_piece.shape[0]
    block_rows = math.gcd(piece_rows, 512)
    block_count = piece_rows // block_rows
    key_blocks = key_piece.reshape(block_count, block_rows, head_count, KEY_SIZE)
    value_blocks = value_piece.reshape(block_count, block_rows, head_count, VALUE_SIZE)

    def one_block(state, blocks):
        running_max, running_sum, weighted = state
        key_block, value_block = blocks
        scores = (
            jnp.einsum("qhd,khd->hqk", queries, key_block, preferred_element_type=jnp.float32)
            * scale
        )
        new_max = jnp.maximum(running_max, jnp.max(scores, axis=-1))
        shrink = jnp.exp(running_max - new_max)
        weights = jnp.exp(scores - new_max[:, :, None])
        running_sum = running_sum * shrink + jnp.sum(weights, axis=-1)
        update = jnp.einsum(
            "hqk,khd->hqd",
            weights.astype(jnp.bfloat16),
            value_block,
            preferred_element_type=jnp.float32,
        )
        weighted = weighted * shrink[:, :, None] + update
        return ((new_max, running_sum, weighted), None)

    carried, unused = lax.scan(one_block, carried, (key_blocks, value_blocks))
    running_max, running_sum, weighted = carried
    attended = (weighted / running_sum[:, :, None]).astype(jnp.bfloat16)
    attended = attended.transpose(1, 0, 2).reshape(local_rows, head_count * VALUE_SIZE)
    mixed = lax.psum_scatter(
        jnp.dot(attended, w_out, preferred_element_type=jnp.float32).astype(jnp.bfloat16),
        "pair",
        scatter_dimension=0,
        tiled=True,
    ).astype(jnp.float32)
    seq_out = (first_out.astype(jnp.float32) + mixed).astype(jnp.bfloat16)
    bin_count = row_count // POOL
    pooled = jnp.mean(seq_out.astype(jnp.float32).reshape(bin_count, POOL, channels), axis=1)
    bin_norm = norm_rows(pooled, gain_pool).astype(jnp.bfloat16)
    sides = jnp.dot(bin_norm, w_pair, preferred_element_type=jnp.float32).astype(jnp.bfloat16)
    left_side = sides[:, :PAIR_CH]
    right_side = sides[:, PAIR_CH:]
    tile_rows = bin_count * pair_count
    tile_cols = bin_count * seq_count
    row_side = lax.all_gather(left_side, "pair", axis=0, tiled=True)
    all_right = lax.all_gather(right_side, ("seq", "pair"), axis=0, tiled=True)
    column_side = lax.dynamic_slice_in_dim(
        all_right, lax.axis_index("pair") * tile_cols, tile_cols, 0
    )
    pair_tile = (
        row_side.astype(jnp.float32)[:, None, :] * column_side.astype(jnp.float32)[None, :, :]
    ).astype(jnp.bfloat16)
    flat_rows = pair_tile.reshape(tile_rows * tile_cols, PAIR_CH)
    hidden = jax.nn.relu(jnp.dot(flat_rows, w_up, preferred_element_type=jnp.float32)).astype(
        jnp.bfloat16
    )
    pair_out = flat_rows.astype(jnp.float32) + jnp.dot(
        hidden, w_down, preferred_element_type=jnp.float32
    )
    pair_map = pair_out.astype(jnp.bfloat16).reshape(tile_rows, tile_cols, PAIR_CH)
    return (seq_out, pair_map)


def solution(mesh):
    return jax.shard_map(
        shards,
        mesh=mesh,
        in_specs=(
            P(("groups", "seq", "pair"), None),
            P(),
            P(None, "pair", None),
            P(),
            P(None, "pair"),
            P("pair", None),
            P(),
            P(),
            P(),
            P(),
        ),
        out_specs=(P(("groups", "seq", "pair"), None), P(("groups", "seq"), "pair", None)),
        check_vma=False,
    )
```

profile of v0, /device:TPU:0, one launch (start us, length us, event | category | flops | bytes accessed | tf_op | source)
XLA Modules:
  0.0 302.2 jit_solution(12201782446949053224)
XLA Ops:
  9.8 17.8 %all_to_all.19 = bf16[128,4,384]{2,0,1:T(8,128)(2,1)S(1)} all-to-all(bf16[128,4,384]{2,0,1:T(8,128)(2,1)S(1)} %bitcast.84), channel_id=1, replica_groups=mesh['groups'=2,'seq'=4,'pair'=4] {'pair'}, dimensions={1} | all-to-all | bytes 786432 | tf_op jit(solution)/shard_map/all_to_all | solution.py:50
  27.6 1.5 collective-permute-start
  29.1 2.4 fusion.19
  33.8 2.4 collective-permute-done.1
  38.1 2.6 fusion.10
  40.8 60.6 %reduce-scatter.3.cloned.1.call-done = f32[128,1536]{1,0:T(8,128)} async-done(((f32[512,1536]{1,0:T(8,128)}), f32[128,1536]{1,0:T(8,128)}) %reduce-scatter.3.cloned.1.call-update) | async-done | bytes 786448 | tf_op jit(solution)/shard_map/reduce_scatter | solution.py:52
  104.5 37.2 %all-gather.4.cloned.1.call-done = bf16[512,1536]{1,0:T(8,128)(2,1)} async-done(((bf16[128,1536]{1,0:T(8,128)(2,1)}), bf16[512,1536]{1,0:T(8,128)(2,1)}) %all-gather.4.cloned.1.call-update) | async-done | bytes 1572880 | tf_op jit(solution)/shard_map/all_gather | solution.py:61
  141.7 3.7 %convolution_convert_fusion.1 = bf16[512,768]{1,0:T(8,128)(2,1)} fusion(bf16[512,1536]{1,0:T(8,128)(2,1)} %all-gather.4.cloned.1.call-done, bf16[1536,768]{1,0:T(8,128)(2,1)S(1)} %copy-done), kind=kOutput, calls=%fused_computation.25 | convolution fusion | flops 1208352768 | bytes 4718592 | tf_op jit(solution)/shard_map/dot_general | solution.py:60
  145.4 2.1 reshape.71
  149.5 1.7 copy.43
  151.3 13.8 %all-gather.6.cloned.1.call-done = bf16[2048,256]{1,0:T(8,128)(2,1)} async-done(((bf16[512,256]{1,0:T(8,128)(2,1)}), bf16[2048,256]{1,0:T(8,128)(2,1)}) %all-gather.6.cloned.1.call-update) | async-done | bytes 1048592 | tf_op jit(solution)/shard_map/all_gather | solution.py:77
  165.2 2.2 reshape.73
  167.3 16.0 %all-gather.8.cloned.1.call-done = bf16[2048,256]{1,0:T(8,128)(2,1)} async-done(((bf16[512,256]{1,0:T(8,128)(2,1)}), bf16[2048,256]{1,0:T(8,128)(2,1)}) %all-gather.8.cloned.1.call-update) | async-done | bytes 1048592 | tf_op jit(solution)/shard_map/all_gather | solution.py:78
  183.3 2.2 reshape.75
  185.5 24.8 %while.15 = (s32[]{:T(128)}, f32[2,512]{1,0:T(2,128)S(1)}, f32[2,512]{1,0:T(2,128)S(1)}, f32[2,512,128]{2,1,0:T(8,128)S(1)}, bf16[4,512,2,128]{3,2,1,0:T(2,128)(...) while((s32[]{:T(128)}, f32[2,512]{1,0:T(2,128)S(1)}, ...), condition=%wide.region_6.7_spmd.clone, body=%wide.region_3.6_spmd.clone.sunk | while | flops 273028096 | bytes 17629320 | solution.py:105
  186.9 1.8 bitcast_reduce_fusion.2
  188.7 2.1 fusion.74
  191.7 1.4 constant_dynamic-slice_fusion.3
  193.1 1.8 bitcast_reduce_fusion.2
  194.9 2.1 fusion.74
  197.9 1.4 constant_dynamic-slice_fusion.3
  199.3 1.8 bitcast_reduce_fusion.2
  201.1 2.1 fusion.74
  204.1 1.4 constant_dynamic-slice_fusion.3
  205.5 1.8 bitcast_reduce_fusion.2
  207.3 2.1 fusion.74
  210.6 3.0 convolution_convert_fusion
  213.6 35.4 %reduce-scatter.5.cloned.1.call-done = bf16[128,1536]{1,0:T(8,128)(2,1)} async-done(((bf16[512,1536]{1,0:T(8,128)(2,1)}), bf16[128,1536]{1,0:T(8,128)(2,1)}) %reduce-scatter.5.cloned.1.call-update) | async-done | bytes 393232 | tf_op jit(solution)/shard_map/reduce_scatter | solution.py:109
  249.1 1.8 convert_reduce_fusion
  251.3 30.4 %all_gather.19 = bf16[128,128]{1,0:T(8,128)(2,1)S(1)} all-gather(bf16[8,128]{1,0:T(8,128)(2,1)S(1)} %get-tuple-element.110), channel_id=1, replica_groups=mesh['groups'=2,'seq'=4,'pair'=4] {'seq','pair'}, dimensions={0}, use_global_device_ids=true | all-gather | bytes 34816 | tf_op jit(solution)/shard_map/all_gather | solution.py:125
  281.7 11.9 %all_gather.18 = bf16[32,128]{1,0:T(8,128)(2,1)S(1)} all-gather(bf16[8,128]{1,0:T(8,128)(2,1)S(1)} %get-tuple-element.109), channel_id=1, replica_groups=mesh['groups'=2,'seq'=4,'pair'=4] {'pair'}, dimensions={0}, use_global_device_ids=true | all-gather | bytes 10240 | tf_op jit(solution)/shard_map/all_gather | solution.py:124
  293.6 2.1 fusion.15
  (79 shorter events, 17.8 us)
Async XLA Ops:
  7.2 134.5 %copy-start = (bf16[1536,768]{1,0:T(8,128)(2,1)S(1)}, bf16[1536,768]{1,0:T(8,128)(2,1)}, u32[]{:S(2)}) copy-start(bf16[1536,768]{1,0:T(8,128)(2,1)} %param.16) | copy-start | bytes 7077892
  7.2 94.2 %reduce-scatter.3.cloned.1.call-start = ((), (), s32[]{:S(2)}) async-start(), calls=%async_computation.3 | async-start | bytes 3932160 | tf_op jit(solution)/shard_map/reduce_scatter | solution.py:52
  27.6 5.3 %copy-start.2 = (bf16[5,384,1536]{2,1,0:T(8,128)(2,1)S(1)}, bf16[5,384,1536]{2,1,0:T(8,128)(2,1)}, u32[]{:S(2)}) copy-start(bf16[5,384,1536]{2,1,0:T(8,128)(2,1)} %param.14) | copy-start | bytes 17694724
  27.6 5.3 %collective-permute-start = (bf16[8,384]{1,0:T(8,128)(2,1)S(1)}, bf16[8,384]{1,0:T(8,128)(2,1)S(1)}, u32[]{:S(2)}, u32[]{:S(2)}) collective-permute-start(bf16[8,384]{1,0:T(8,128)(2,1)S(1)} %get-tuple-element.107), channel_id=1, source_target_pairs={{0,4},{4,8},{8,12},{1,5},{5,9},{9,13},{2,6},{6,10},{10,14},{3,7},{... | collective-permute-start | bytes 18440 | tf_op jit(solution)/shard_map/ppermute | solution.py:22
  31.5 4.7 %collective-permute-start.1 = (bf16[8,384]{1,0:T(8,128)(2,1)S(1)}, bf16[8,384]{1,0:T(8,128)(2,1)S(1)}, u32[]{:S(2)}, u32[]{:S(2)}) collective-permute-start(bf16[8,384]{1,0:T(8,128)(2,1)S(1)} %get-tuple-element.108), channel_id=1, source_target_pairs={{4,0},{8,4},{12,8},{5,1},{9,5},{13,9},{6,2},{10,6},{14,10},{7,3},{... | collective-permute-start | bytes 18440 | tf_op jit(solution)/shard_map/ppermute | solution.py:23
  40.8 60.6 %copy-start.3 = (bf16[128,1536]{1,0:T(8,128)(2,1)S(1)}, bf16[128,1536]{1,0:T(8,128)(2,1)}, u32[]{:S(2)}) copy-start(bf16[128,1536]{1,0:T(8,128)(2,1)} %param.12) | copy-start | bytes 1179652
  40.8 62.7 %copy-start.7 = (f32[1536]{0:T(1024)S(1)}, f32[1536]{0:T(1024)}, u32[]{:S(2)}) copy-start(f32[1536]{0:T(1024)} %param.15) | copy-start | bytes 18436
  40.8 100.9 %all-gather.4.cloned.1.call-start = ((), (), s32[]{:S(2)}) async-start(), calls=%async_computation.4 | async-start | bytes 1966080 | tf_op jit(solution)/shard_map/all_gather | solution.py:61
  102.7 0.8 copy-start.4
  104.4 60.7 %all-gather.6.cloned.1.call-start = ((), (), s32[]{:S(2)}) async-start(), calls=%async_computation.5 | async-start | bytes 1310720 | tf_op jit(solution)/shard_map/all_gather | solution.py:77
  149.4 33.9 %all-gather.8.cloned.1.call-start = ((), (), s32[]{:S(2)}) async-start(), calls=%async_computation.6 | async-start | bytes 1310720 | tf_op jit(solution)/shard_map/all_gather | solution.py:78
  151.2 97.9 %reduce-scatter.5.cloned.1.call-start = ((), (), s32[]{:S(2)}) async-start(), calls=%async_computation.7 | async-start | bytes 1966080 | tf_op jit(solution)/shard_map/reduce_scatter | solution.py:109
  188.7 2.2 copy-start.1
  194.9 2.2 copy-start.1
  201.1 2.2 copy-start.1
  207.3 2.2 copy-start.1
  210.5 38.5 %copy-start.5 = (bf16[128,1536]{1,0:T(8,128)(2,1)S(1)}, bf16[128,1536]{1,0:T(8,128)(2,1)}, u32[]{:S(2)}) copy-start(bf16[128,1536]{1,0:T(8,128)(2,1)} %copy-done.4) | copy-start | bytes 1179652
  210.6 40.4 %copy-start.6 = (bf16[1536,256]{1,0:T(8,128)(2,1)S(1)}, bf16[1536,256]{1,0:T(8,128)(2,1)}, u32[]{:S(2)}) copy-start(bf16[1536,256]{1,0:T(8,128)(2,1)} %param.19) | copy-start | bytes 2359300
  210.6 40.4 %copy-start.8 = (f32[1536]{0:T(1024)S(1)}, f32[1536]{0:T(1024)}, u32[]{:S(2)}) copy-start(f32[1536]{0:T(1024)} %param.18) | copy-start | bytes 18436
Sparse Core Ops, SparseCore 0:
  40.9 60.4 reduce-scatter.2
  104.5 37.0 all-gather.3
  149.5 15.5 all-gather.5
  166.6 16.7 all-gather.7
  213.7 35.2 reduce-scatter.4
where the time goes:
time: 303 us; the launch traced here: 302 us
  waiting for transfers between devices  166 us (55%)
  blocking collectives  60 us (20%)
  matrix products  27.2 us (9%)
  local copies, waits for them, and re-layouts  17.1 us (6%)
  other arithmetic  15.3 us (5%)
  between operations  14 us (5%)
  starting transfers between devices  3.04 us (1%)
    reduce_scatter x1, waiting for transfers between devices, shards(): lax.psum_scatter(conv_rows(padded, conv_weight, row_count * lax.axis_size...  60.6 us
    all_gather x1, waiting for transfers between devices, shards(): lax.all_gather(attn_in, 'pair', axis=0, tiled=True)  37.2 us
    reduce_scatter x1, waiting for transfers between devices, shards(): lax.psum_scatter(jnp.dot(attended, w_out, preferred_element_type=jnp.floa...  35.4 us
    all_gather x1, blocking collectives, shards(): all_right = lax.all_gather(right_side, ('seq', 'pair'), axis=0, tiled=True)  30.4 us
    all_to_all x1, blocking collectives, shards(): lax.all_to_all(normed, 'pair', split_axis=1, concat_axis=0, tiled=True)  17.8 us
    all_gather x1, waiting for transfers between devices, shards(): value_piece = lax.all_gather(value_rows, 'seq', axis=0, tiled=True)  16 us
    all_gather x1, waiting for transfers between devices, shards(): key_piece = lax.all_gather(key_rows, 'seq', axis=0, tiled=True)  13.8 us
    all_gather x1, blocking collectives, shards(): row_side = lax.all_gather(left_side, 'pair', axis=0, tiled=True)  11.9 us
  transfers between devices with their start and end apart: 7, of which 6 were waited for; matrix products, arithmetic and copies ran while one was open for 2% of the time, Pallas kernels for 0%

commit v1 on v0

--- a/solution.py
+++ b/solution.py
@@ -74,8 +74,12 @@
         jnp.zeros((head_count, local_rows, VALUE_SIZE), jnp.float32),
     )
     carried = start_state
-    key_piece = lax.all_gather(key_rows, "seq", axis=0, tiled=True)
-    value_piece = lax.all_gather(value_rows, "seq", axis=0, tiled=True)
+    connect_pools_here = lambda a0, obj, mesh_ax: jnp.split(
+        lax.all_gather(jnp.concatenate([a0, obj], axis=1), mesh_ax, axis=0, tiled=True),
+        [a0.shape[1]],
+        axis=1,
+    )
+    key_piece, value_piece = connect_pools_here(key_rows, value_rows, "seq")
     piece_rows = key_piece.shape[0]
     block_rows = math.gcd(piece_rows, 512)
     block_count = piece_rows // block_rows

time: 303 us -> 295 us (0.974)
  waiting for transfers between devices: 166 us -> 157 us
    all_gather x2 -> x1, waiting for transfers between devices: 29.9 us -> 21.5 us  [shards(): lax.all_gather(jnp.concatenate([a0, obj], axis=1), mesh_ax, axis=0, tiled...]
  transfers between devices with their start and end apart: 7 -> 6, of which waited for: 6 -> 5; matrix products, arithmetic and copies ran while one was open for 2% -> 1% of each run, Pallas kernels for 0% -> 0%
where the time goes in v1:
time: 295 us
  waiting for transfers between devices  157 us (53%)
  blocking collectives  60 us (20%)
  matrix products  27.3 us (9%)
  local copies, waits for them, and re-layouts  17 us (6%)
  other arithmetic  16.2 us (5%)
  between operations  14 us (5%)
  starting transfers between devices  3 us (1%)
    reduce_scatter x1, waiting for transfers between devices, shards(): lax.psum_scatter(conv_rows(padded, conv_weight, row_count * lax.axis_size...  60.6 us
    all_gather x1, waiting for transfers between devices, shards(): lax.all_gather(attn_in, 'pair', axis=0, tiled=True)  37.2 us
    reduce_scatter x1, waiting for transfers between devices, shards(): lax.psum_scatter(jnp.dot(attended, w_out, preferred_element_type=jnp.floa...  35.4 us
    all_gather x1, blocking collectives, shards(): all_right = lax.all_gather(right_side, ('seq', 'pair'), axis=0, tiled=True)  30.4 us
    all_gather x1, waiting for transfers between devices, shards(): lax.all_gather(jnp.concatenate([a0, obj], axis=1), mesh_ax, axis=0, tiled...  21.5 us
    all_to_all x1, blocking collectives, shards(): lax.all_to_all(normed, 'pair', split_axis=1, concat_axis=0, tiled=True)  17.8 us
    all_gather x1, blocking collectives, shards(): row_side = lax.all_gather(left_side, 'pair', axis=0, tiled=True)  11.9 us
    reduce_sum x4, other arithmetic, one_block(): running_sum = running_sum * shrink + jnp.sum(weights, axis=-1)  8.4 us
  transfers between devices with their start and end apart: 6, of which 5 were waited for; matrix products, arithmetic and copies ran while one was open for 1% of the time, Pallas kernels for 0%

profile of v1, /device:TPU:0, one launch (start us, length us, event | category | flops | bytes accessed | tf_op | source)
XLA Modules:
  0.0 294.7 jit_solution(15376484793078136844)
XLA Ops:
  9.8 17.8 %all_to_all.19 = bf16[128,4,384]{2,0,1:T(8,128)(2,1)S(1)} all-to-all(bf16[128,4,384]{2,0,1:T(8,128)(2,1)S(1)} %bitcast.82), channel_id=1, replica_groups=mesh['groups'=2,'seq'=4,'pair'=4] {'pair'}, dimensions={1} | all-to-all | bytes 786432 | tf_op jit(solution)/shard_map/all_to_all | solution.py:50
  27.6 1.5 collective-permute-start
  29.1 2.4 fusion.19
  33.8 2.4 collective-permute-done.1
  38.1 2.6 fusion.10
  40.8 60.6 %reduce-scatter.3.cloned.1.call-done = f32[128,1536]{1,0:T(8,128)} async-done(((f32[512,1536]{1,0:T(8,128)}), f32[128,1536]{1,0:T(8,128)}) %reduce-scatter.3.cloned.1.call-update) | async-done | bytes 786448 | tf_op jit(solution)/shard_map/reduce_scatter | solution.py:52
  104.5 37.2 %all-gather.3.cloned.1.call-done = bf16[512,1536]{1,0:T(8,128)(2,1)} async-done(((bf16[128,1536]{1,0:T(8,128)(2,1)}), bf16[512,1536]{1,0:T(8,128)(2,1)}) %all-gather.3.cloned.1.call-update) | async-done | bytes 1572880 | tf_op jit(solution)/shard_map/all_gather | solution.py:61
  141.7 3.7 %convolution_convert_fusion.1 = bf16[512,768]{1,0:T(8,128)(2,1)} fusion(bf16[512,1536]{1,0:T(8,128)(2,1)} %all-gather.3.cloned.1.call-done, bf16[1536,768]{1,0:T(8,128)(2,1)S(1)} %copy-done), kind=kOutput, calls=%fused_computation.25 | convolution fusion | flops 1208352768 | bytes 4718592 | tf_op jit(solution)/shard_map/dot_general | solution.py:60
  145.4 2.1 reshape.71
  149.1 21.5 %all-gather.5.cloned.1.call-done = bf16[2048,512]{1,0:T(8,128)(2,1)} async-done(((bf16[512,512]{1,0:T(8,128)(2,1)}), bf16[2048,512]{1,0:T(8,128)(2,1)}) %all-gather.5.cloned.1.call-update) | async-done | bytes 2097168 | tf_op jit(solution)/shard_map/all_gather | solution.py:78
  170.6 3.0 %fusion.53 = (bf16[2048,256]{1,0:T(8,128)(2,1)}, bf16[2048,256]{1,0:T(8,128)(2,1)}) fusion(bf16[2048,512]{1,0:T(8,128)(2,1)} %all-gather.5.cloned.1.call-done), kind=kLoop, calls=%fused_computation.90 | loop fusion | bytes 4194304 | tf_op jit(solution)/shard_map/split | solution.py:77
  173.6 2.2 reshape.74
  175.7 2.1 reshape.75
  177.9 24.9 %while.15 = (s32[]{:T(128)}, f32[2,512]{1,0:T(2,128)S(1)}, f32[2,512]{1,0:T(2,128)S(1)}, f32[2,512,128]{2,1,0:T(8,128)S(1)}, bf16[4,512,2,128]{3,2,1,0:T(2,128)(...) while((s32[]{:T(128)}, f32[2,512]{1,0:T(2,128)S(1)}, ...), condition=%wide.region_6.7_spmd.clone, body=%wide.region_3.6_spmd.clone.sunk | while | flops 273028096 | bytes 17629320 | solution.py:109
  177.9 1.4 constant_dynamic-slice_fusion.3
  179.3 1.8 bitcast_reduce_fusion.2
  181.0 2.1 fusion.75
  184.1 1.4 constant_dynamic-slice_fusion.3
  185.5 1.8 bitcast_reduce_fusion.2
  187.3 2.1 fusion.75
  190.3 1.4 constant_dynamic-slice_fusion.3
  191.7 1.8 bitcast_reduce_fusion.2
  193.5 2.1 fusion.75
  196.5 1.4 constant_dynamic-slice_fusion.3
  197.9 1.8 bitcast_reduce_fusion.2
  199.7 2.1 fusion.75
  203.0 3.0 %convolution_convert_fusion = bf16[512,1536]{1,0:T(8,128)(2,1)} fusion(bf16[512,256]{0,1:T(8,128)(2,1)S(1)} %bitcast.84, bf16[256,1536]{1,0:T(8,128)(2,1)} %param.17), kind=kOutput, calls=%fused_computation.24 | convolution fusion | flops 403439616 | bytes 2621440 | tf_op jit(solution)/shard_map/dot_general | solution.py:114
  206.0 35.4 %reduce-scatter.5.cloned.1.call-done = bf16[128,1536]{1,0:T(8,128)(2,1)} async-done(((bf16[512,1536]{1,0:T(8,128)(2,1)}), bf16[128,1536]{1,0:T(8,128)(2,1)}) %reduce-scatter.5.cloned.1.call-update) | async-done | bytes 393232 | tf_op jit(solution)/shard_map/reduce_scatter | solution.py:113
  241.5 1.8 convert_reduce_fusion
  243.7 30.4 %all_gather.15 = bf16[128,128]{1,0:T(8,128)(2,1)S(1)} all-gather(bf16[8,128]{1,0:T(8,128)(2,1)S(1)} %get-tuple-element.112), channel_id=1, replica_groups=mesh['groups'=2,'seq'=4,'pair'=4] {'seq','pair'}, dimensions={0}, use_global_device_ids=true | all-gather | bytes 34816 | tf_op jit(solution)/shard_map/all_gather | solution.py:129
  274.1 11.9 %all_gather.14 = bf16[32,128]{1,0:T(8,128)(2,1)S(1)} all-gather(bf16[8,128]{1,0:T(8,128)(2,1)S(1)} %get-tuple-element.111), channel_id=1, replica_groups=mesh['groups'=2,'seq'=4,'pair'=4] {'pair'}, dimensions={0}, use_global_device_ids=true | all-gather | bytes 10240 | tf_op jit(solution)/shard_map/all_gather | solution.py:128
  286.0 2.1 fusion.15
  (77 shorter events, 15.9 us)
Async XLA Ops:
  7.2 134.6 %copy-start = (bf16[1536,768]{1,0:T(8,128)(2,1)S(1)}, bf16[1536,768]{1,0:T(8,128)(2,1)}, u32[]{:S(2)}) copy-start(bf16[1536,768]{1,0:T(8,128)(2,1)} %param.16) | copy-start | bytes 7077892
  7.2 94.2 %reduce-scatter.3.cloned.1.call-start = ((), (), s32[]{:S(2)}) async-start(), calls=%async_computation.3 | async-start | bytes 3932160 | tf_op jit(solution)/shard_map/reduce_scatter | solution.py:52
  27.6 5.3 %copy-start.2 = (bf16[5,384,1536]{2,1,0:T(8,128)(2,1)S(1)}, bf16[5,384,1536]{2,1,0:T(8,128)(2,1)}, u32[]{:S(2)}) copy-start(bf16[5,384,1536]{2,1,0:T(8,128)(2,1)} %param.14) | copy-start | bytes 17694724
  27.6 5.3 %collective-permute-start = (bf16[8,384]{1,0:T(8,128)(2,1)S(1)}, bf16[8,384]{1,0:T(8,128)(2,1)S(1)}, u32[]{:S(2)}, u32[]{:S(2)}) collective-permute-start(bf16[8,384]{1,0:T(8,128)(2,1)S(1)} %get-tuple-element.109), channel_id=1, source_target_pairs={{0,4},{4,8},{8,12},{1,5},{5,9},{9,13},{2,6},{6,10},{10,14},{3,7},{... | collective-permute-start | bytes 18440 | tf_op jit(solution)/shard_map/ppermute | solution.py:22
  31.5 4.7 %collective-permute-start.1 = (bf16[8,384]{1,0:T(8,128)(2,1)S(1)}, bf16[8,384]{1,0:T(8,128)(2,1)S(1)}, u32[]{:S(2)}, u32[]{:S(2)}) collective-permute-start(bf16[8,384]{1,0:T(8,128)(2,1)S(1)} %get-tuple-element.110), channel_id=1, source_target_pairs={{4,0},{8,4},{12,8},{5,1},{9,5},{13,9},{6,2},{10,6},{14,10},{7,3},{... | collective-permute-start | bytes 18440 | tf_op jit(solution)/shard_map/ppermute | solution.py:23
  40.8 60.6 %copy-start.3 = (bf16[128,1536]{1,0:T(8,128)(2,1)S(1)}, bf16[128,1536]{1,0:T(8,128)(2,1)}, u32[]{:S(2)}) copy-start(bf16[128,1536]{1,0:T(8,128)(2,1)} %param.12) | copy-start | bytes 1179652
  40.8 62.8 %copy-start.7 = (f32[1536]{0:T(1024)S(1)}, f32[1536]{0:T(1024)}, u32[]{:S(2)}) copy-start(f32[1536]{0:T(1024)} %param.15) | copy-start | bytes 18436
  40.8 100.9 %all-gather.3.cloned.1.call-start = ((), (), s32[]{:S(2)}) async-start(), calls=%async_computation.4 | async-start | bytes 1966080 | tf_op jit(solution)/shard_map/all_gather | solution.py:61
  102.7 0.8 copy-start.4
  104.5 66.1 %all-gather.5.cloned.1.call-start = ((), (), s32[]{:S(2)}) async-start(), calls=%async_computation.5 | async-start | bytes 2621440 | tf_op jit(solution)/shard_map/all_gather | solution.py:78
  149.0 92.5 %reduce-scatter.5.cloned.1.call-start = ((), (), s32[]{:S(2)}) async-start(), calls=%async_computation.6 | async-start | bytes 1966080 | tf_op jit(solution)/shard_map/reduce_scatter | solution.py:113
  181.0 2.2 copy-start.1
  187.3 2.2 copy-start.1
  193.5 2.2 copy-start.1
  199.7 2.2 copy-start.1
  203.0 38.5 %copy-start.5 = (bf16[128,1536]{1,0:T(8,128)(2,1)S(1)}, bf16[128,1536]{1,0:T(8,128)(2,1)}, u32[]{:S(2)}) copy-start(bf16[128,1536]{1,0:T(8,128)(2,1)} %copy-done.4) | copy-start | bytes 1179652
  203.0 40.5 %copy-start.6 = (bf16[1536,256]{1,0:T(8,128)(2,1)S(1)}, bf16[1536,256]{1,0:T(8,128)(2,1)}, u32[]{:S(2)}) copy-start(bf16[1536,256]{1,0:T(8,128)(2,1)} %param.19) | copy-start | bytes 2359300
  203.0 40.5 %copy-start.8 = (f32[1536]{0:T(1024)S(1)}, f32[1536]{0:T(1024)}, u32[]{:S(2)}) copy-start(f32[1536]{0:T(1024)} %param.18) | copy-start | bytes 18436
Sparse Core Ops, SparseCore 0:
  40.9 60.4 reduce-scatter.2
  104.6 37.1 all-gather.2
  149.1 21.4 all-gather.4
  206.2 35.2 reduce-scatter.4
